TPU v7x, 32 devices: a whole 2x2x4 slice. The times are simulated.
32 devices in a mesh: users: 16 (over z, y, core), items: 2 (over x).
Axes of the slice: x: 2, y: 2, z: 4, core: 2. Of those that a mesh axis runs over, the one named last changes fastest.
Arguments:
- ratings: bfloat16 [64, 6, 128, 128], P('users', 'items')
- residual: bfloat16 [64, 6, 128, 128], P('users', 'items')
- tile_columns: int32 [64, 6], P('users', 'items'), may hold values from 0 to 2, as said below
- occupied: int32 [64, 6], P('users', 'items'), may hold values from 0 to 1, as said below
- chosen: int32 [64], P('users'), may hold values from 0 to 1, as said below
- user_factors: bfloat16 [64, 8192], P(None, 'users'), may hold values from -5 to 5
- item_factors: bfloat16 [2, 64, 384], P('items'), may hold values from -5 to 5
- start_block: bfloat16 [2, 32, 384], P('items'), may hold values from -0.5 to 0.5
Outputs:
- updated: bfloat16 [64, 6, 128, 128], P('users', 'items')
- left_block: float32 [32, 8192], P(None, 'users')
- right_block: float32 [2, 32, 384], P('items')
Inputs may be any that keep to these rules, and one draw needn't show every extreme that they name: `tile_columns`: within one tile row and one item block the 3 slots name different tile columns. Within one tile row and one item block the occupied slots come first, at least one is occupied, and some tile rows have all 3 occupied. Exactly 16 tile rows are chosen.
All inputs are finite; a program needn't handle non-finite values.
Results may differ from a plain program's by a relative error of at most 0.0033.
Values sent between devices are 32-bit elements; how exact they have to be, the bound alone decides.
No kernel may reach another device: no remote copies, remote signals or barrier semaphores. Data moves between devices by JAX's collectives and lax.ppermute only.
A program may use at most 64 MiB of HBM per device.

v0:
```python
import jax
import jax.numpy as jnp
from jax import lax
from jax.sharding import PartitionSpec as P


def local(
    ratings, residual, tile_columns, occupied, chosen, user_factors, item_factors, start_block
):
    rows_dev = ratings.shape[0]
    width = ratings.shape[2]
    rank_size = user_factors.shape[0]
    block_size = start_block.shape[1]
    item_count = item_factors.shape[2] // width
    user_total = user_factors.shape[1] * lax.axis_size("users")
    root = float(user_total) ** 0.5
    item_tiles = item_factors[0].reshape(rank_size, item_count, width)
    factors = jnp.take(item_tiles, tile_columns, axis=1)
    user_tiles = user_factors.reshape(rank_size, rows_dev, width)
    estimate = jnp.einsum("rta,rtkb->tkab", user_tiles, factors, preferred_element_type=jnp.float32)
    live_slot = (occupied > 0)[:, :, None, None]
    selected = live_slot & (chosen > 0)[:, None, None, None]
    updated = jnp.where(
        selected, ratings.astype(jnp.float32) - estimate, residual.astype(jnp.float32)
    )
    updated = jnp.where(live_slot, updated, jnp.float32(0.0)).astype(jnp.bfloat16)
    start_tiles = jnp.take(
        start_block[0].reshape(block_size, item_count, width), tile_columns, axis=1
    )
    partial_products = jnp.einsum(
        "tkab,jtkb->jta", updated, start_tiles, preferred_element_type=jnp.float32
    )
    partial_products = partial_products.reshape(block_size, rows_dev * width)
    share = lax.psum_scatter(partial_products, "items", scatter_dimension=1, tiled=True)
    gram_part = jnp.dot(share, share.T, precision=lax.Precision.HIGHEST)
    gram = lax.psum(gram_part, ("users", "items")) / user_total
    lower = jnp.linalg.cholesky(gram)
    left_share = jax.scipy.linalg.solve_triangular(lower, share, lower=True)
    left_block = lax.all_gather(left_share, "items", axis=1, tiled=True)
    left_rounded = left_block.astype(jnp.bfloat16).reshape(block_size, rows_dev, width)
    slot_terms = jnp.einsum(
        "tkab,jta->jtkb", updated, left_rounded, preferred_element_type=jnp.float32
    )
    one_hot = (
        tile_columns[:, :, None] == jnp.arange(item_count, dtype=jnp.int32)[None, None, :]
    ).astype(jnp.float32)
    item_terms = jnp.einsum("jtkb,tkc->jcb", slot_terms, one_hot, precision=lax.Precision.HIGHEST)
    item_terms = item_terms.reshape(1, block_size, item_count * width)
    summed = lax.psum(item_terms, "users")
    start_term = jnp.einsum(
        "ji,bjn->bin", lower, start_block.astype(jnp.float32), precision=lax.Precision.HIGHEST
    )
    right_block = summed / root - root * start_term
    return (updated, left_block, right_block)


def solution(mesh):
    placed = (
        P("users", "items", None, None),
        P("users", "items", None, None),
        P("users", "items"),
        P("users", "items"),
        P("users"),
        P(None, "users"),
        P("items", None, None),
        P("items", None, None),
    )
    return jax.shard_map(
        local,
        mesh=mesh,
        in_specs=placed,
        out_specs=(P("users", "items", None, None), P(None, "users"), P("items", None, None)),
        check_vma=False,
    )
```

profile of v0, /device:TPU:0, one launch (start us, length us, event | category | flops | bytes accessed | tf_op | source)
XLA Modules:
  0.0 148.7 jit_solution(266476572557245708)
XLA Ops:
  7.2 0.7 broadcast_compare_fusion.1
  7.9 0.7 compare_select_fusion
  8.6 0.1 reshape.53
  8.6 0.8 reshape_squeeze.6
  9.5 1.3 copy.21
  10.8 0.2 copy.24
  11.0 0.6 copy-done.3
  11.6 0.7 copy-done.2
  12.4 0.6 gather_fusion
  13.0 0.6 gather_fusion.1
  13.6 0.1 copy-done.4
  13.7 0.1 broadcast_and_fusion
  13.8 0.5 fusion.3
  14.2 0.2 convolution_bitcast_fusion.2
  14.5 0.6 copy.51
  15.1 0.1 copy.30
  15.2 0.9 copy.31
  16.1 11.7 %reduce-scatter.2.cloned.1.call-done = f32[32,256]{1,0:T(8,128)} async-done(((f32[32,512]{1,0:T(8,128)}), f32[32,256]{1,0:T(8,128)}) %reduce-scatter.2.cloned.1.call-update) | async-done | bytes 32784 | tf_op jit(solution)/shard_map/reduce_scatter | solution.py:34
  27.9 1.0 fusion.33
  28.9 39.5 %psum.14 = f32[32,32]{0,1:T(8,128)S(1)} all-reduce(f32[32,32]{0,1:T(8,128)S(1)} %fusion.33), channel_id=1, replica_groups=mesh['users'=16,'items'=2] {'users','items'}, use_global_device_ids=true, to_apply=%region_1.2 | all-reduce | flops 1024 | bytes 8192 | tf_op jit(solution)/shard_map/psum | solution.py:36
  68.3 0.1 copy.29
  68.4 2.9 %cholesky.16 = f32[32,32]{1,0:T(8,128)S(1)} custom-call(f32[32,32]{1,0:T(8,128)S(1)} %fusion.22), custom_call_target="Cholesky" | custom-call | tf_op jit(solution)/shard_map/jit(cholesky)/cholesky | solution.py:37
  71.3 0.6 compare_reduce_fusion
  72.0 0.7 select_bitcast_fusion
  72.7 2.4 %custom-call.7 = f32[1,32,32]{1,2,0:T(8,128)S(1)} custom-call(f32[1,32,32]{2,1,0:T(8,128)S(1)} %select_bitcast_fusion), custom_call_target="InvertDiagBlocksLowerTriangular" | custom-call | tf_op jit(solution)/shard_map/jit(_solve_triangular)/triangular_solve | solution.py:38
  75.1 0.2 fusion.20
  75.3 4.8 %all_gather.3 = f32[32,512]{1,0:T(8,128)S(1)} all-gather(f32[32,256]{1,0:T(8,128)S(1)} %fusion.20), channel_id=1, replica_groups=mesh['users'=16,'items'=2] {'items'}, dimensions={1}, use_global_device_ids=true | all-gather | bytes 98304 | tf_op jit(solution)/shard_map/all_gather | solution.py:39
  80.2 0.2 fusion.17
  80.4 0.4 convolution_bitcast_fusion.1
  80.9 58.8 %psum.15 = f32[1,32,384]{2,1,0:T(8,128)S(1)} all-reduce(f32[1,32,384]{2,1,0:T(8,128)S(1)} %reshape.49), channel_id=1, replica_groups=mesh['users'=16,'items'=2] {'users'}, use_global_device_ids=true, to_apply=%region_4.5 | all-reduce | flops 12288 | bytes 98304 | tf_op jit(solution)/shard_map/psum | solution.py:49
  139.7 1.5 %fusion.5 = f32[1,32,384]{2,1,0:T(8,128)} fusion(f32[1,32,384]{2,1,0:T(8,128)S(1)} %psum.15, bf16[1,32,384]{2,1,0:T(8,128)(2,1)S(1)} %copy-done.2, f32[32,32]{1,0:T(8,128)S(1)} %cholesky.16, pred[]{:T(512)} %compare_reduce_fusion), kind=kOutput, calls=%fused_computation.11 | convolution fusion | flops 4758528 | bytes 126977 | tf_op jit(solution)/shard_map/ji,bjn->bin/dot_general | solution.py:50
  141.2 0.6 copy.53
  (22 shorter events, 0.2 us)
Async XLA Ops:
  7.2 20.7 %reduce-scatter.2.cloned.1.call-start = ((), (), s32[]{:S(2)}) async-start(), calls=%async_computation.1 | async-start | bytes 98304 | tf_op jit(solution)/shard_map/reduce_scatter | solution.py:34
  9.5 1.3 copy-start
  10.8 0.8 copy-start.3
  11.6 0.7 copy-start.2
  13.0 0.7 copy-start.4
  13.0 0.7 copy-start.5
  68.4 6.7 %copy-start.1 = (f32[32,256]{1,0:T(8,128)S(1)}, f32[32,256]{1,0:T(8,128)}, u32[]{:S(2)}) copy-start(f32[32,256]{1,0:T(8,128)} %reduce-scatter.2.cloned.1.call-done) | copy-start | bytes 98308
Sparse Core Ops, SparseCore 0:
  15.2 12.5 reduce-scatter.1
where the time goes:
time: 149 us
  blocking collectives  103 us (69%)
  between operations  14.2 us (10%)
  waiting for transfers between devices  11.7 us (8%)
  other arithmetic  8.12 us (5%)
  local copies, waits for them, and re-layouts  7.45 us (5%)
  matrix products  4.09 us (3%)
    psum x1, blocking collectives, local(): summed = lax.psum(item_terms, 'users')  58.8 us
    psum x1, blocking collectives, local(): gram = lax.psum(gram_part, ('users', 'items')) / user_total  39.5 us
    reduce_scatter x1, waiting for transfers between devices, local(): lax.psum_scatter(partial_products, 'items', scatter_dimension=1, tiled=True)  11.7 us
    all_gather x1, blocking collectives, local(): left_block = lax.all_gather(left_share, 'items', axis=1, tiled=True)  4.82 us
    unnamed x17, local copies, waits for them, and re-layouts  4.58 us
    another operation x3, other arithmetic, local(): lower = jnp.linalg.cholesky(gram)  3.59 us
    another operation x2, other arithmetic, local(): left_share = jax.scipy.linalg.solve_triangular(lower, share, lower=True)  3.09 us
  transfers between devices with their start and end apart: 1, of which 1 were waited for; matrix products, arithmetic and copies ran while one was open for 1% of the time, Pallas kernels for 0%

commit v1 on v0

--- a/solution.py
+++ b/solution.py
@@ -33,7 +33,7 @@
     partial_products = partial_products.reshape(block_size, rows_dev * width)
     share = lax.psum_scatter(partial_products, "items", scatter_dimension=1, tiled=True)
     gram_part = jnp.dot(share, share.T, precision=lax.Precision.HIGHEST)
-    gram = lax.psum(gram_part, ("users", "items")) / user_total
+    gram = lax.psum(lax.psum(gram_part, "items"), "users") / user_total
     lower = jnp.linalg.cholesky(gram)
     left_share = jax.scipy.linalg.solve_triangular(lower, share, lower=True)
     left_block = lax.all_gather(left_share, "items", axis=1, tiled=True)

time: 149 us -> 174 us (1.17)
  blocking collectives: 103 us -> 128 us
    psum x1 -> x2, blocking collectives: 39.5 us -> 65.9 us  [local(): gram = lax.psum(lax.psum(gram_part, 'items'), 'users') / user_total]
where the time goes in v1:
time: 174 us
  blocking collectives  128 us (74%)
  between operations  14.2 us (8%)
  waiting for transfers between devices  11.7 us (7%)
  other arithmetic  8.12 us (5%)
  local copies, waits for them, and re-layouts  7.45 us (4%)
  matrix products  4.09 us (2%)
    psum x2, blocking collectives, local(): gram = lax.psum(lax.psum(gram_part, 'items'), 'users') / user_total  65.9 us
    psum x1, blocking collectives, local(): summed = lax.psum(item_terms, 'users')  57.7 us
    reduce_scatter x1, waiting for transfers between devices, local(): lax.psum_scatter(partial_products, 'items', scatter_dimension=1, tiled=True)  11.7 us
    all_gather x1, blocking collectives, local(): left_block = lax.all_gather(left_share, 'items', axis=1, tiled=True)  4.59 us
    unnamed x17, local copies, waits for them, and re-layouts  4.58 us
    another operation x3, other arithmetic, local(): lower = jnp.linalg.cholesky(gram)  3.59 us
  transfers between devices with their start and end apart: 1, of which 1 were waited for; matrix products, arithmetic and copies ran while one was open for 1% of the time, Pallas kernels for 0%

profile of v1, /device:TPU:0, one launch (start us, length us, event | category | flops | bytes accessed | tf_op | source)
XLA Modules:
  0.0 173.8 jit_solution(1470335593975007234)
XLA Ops:
  7.2 0.7 broadcast_compare_fusion.1
  7.9 0.7 compare_select_fusion
  8.6 0.1 reshape.53
  8.6 0.8 reshape_squeeze.6
  9.5 1.3 copy.21
  10.8 0.2 copy.24
  11.0 0.6 copy-done.3
  11.6 0.7 copy-done.2
  12.4 0.6 gather_fusion
  13.0 0.6 gather_fusion.1
  13.6 0.1 copy-done.4
  13.8 0.5 fusion.3
  14.2 0.2 convolution_bitcast_fusion.2
  14.5 0.6 copy.51
  15.1 0.1 copy.30
  15.2 0.9 copy.31
  16.1 11.7 %reduce-scatter.2.cloned.1.call-done = f32[32,256]{1,0:T(8,128)} async-done(((f32[32,512]{1,0:T(8,128)}), f32[32,256]{1,0:T(8,128)}) %reduce-scatter.2.cloned.1.call-update) | async-done | bytes 32784 | tf_op jit(solution)/shard_map/reduce_scatter | solution.py:34
  27.9 1.0 fusion.33
  28.9 6.9 %psum.21 = f32[32,32]{0,1:T(8,128)S(1)} all-reduce(f32[32,32]{0,1:T(8,128)S(1)} %fusion.33), channel_id=1, replica_groups=mesh['users'=16,'items'=2] {'items'}, use_global_device_ids=true, to_apply=%region_1.2 | all-reduce | flops 1024 | bytes 8192 | tf_op jit(solution)/shard_map/psum | solution.py:36
  35.7 59.0 %psum.22 = f32[32,32]{0,1:T(8,128)S(1)} all-reduce(f32[32,32]{0,1:T(8,128)S(1)} %psum.21), channel_id=1, replica_groups=mesh['users'=16,'items'=2] {'users'}, use_global_device_ids=true, to_apply=%region_2.3 | all-reduce | flops 1024 | bytes 8192 | tf_op jit(solution)/shard_map/psum | solution.py:36
  94.7 0.1 copy.29
  94.8 2.9 %cholesky.16 = f32[32,32]{1,0:T(8,128)S(1)} custom-call(f32[32,32]{1,0:T(8,128)S(1)} %fusion.22), custom_call_target="Cholesky" | custom-call | tf_op jit(solution)/shard_map/jit(cholesky)/cholesky | solution.py:37
  97.8 0.6 compare_reduce_fusion
  98.4 0.7 select_bitcast_fusion
  99.1 2.4 %custom-call.7 = f32[1,32,32]{1,2,0:T(8,128)S(1)} custom-call(f32[1,32,32]{2,1,0:T(8,128)S(1)} %select_bitcast_fusion), custom_call_target="InvertDiagBlocksLowerTriangular" | custom-call | tf_op jit(solution)/shard_map/jit(_solve_triangular)/triangular_solve | solution.py:38
  101.5 0.2 fusion.20
  101.8 4.6 %all_gather.3 = f32[32,512]{1,0:T(8,128)S(1)} all-gather(f32[32,256]{1,0:T(8,128)S(1)} %fusion.20), channel_id=1, replica_groups=mesh['users'=16,'items'=2] {'items'}, dimensions={1}, use_global_device_ids=true | all-gather | bytes 98304 | tf_op jit(solution)/shard_map/all_gather | solution.py:39
  106.4 0.2 fusion.17
  106.6 0.4 convolution_bitcast_fusion.1
  107.1 57.7 %psum.23 = f32[1,32,384]{2,1,0:T(8,128)S(1)} all-reduce(f32[1,32,384]{2,1,0:T(8,128)S(1)} %reshape.49), channel_id=1, replica_groups=mesh['users'=16,'items'=2] {'users'}, use_global_device_ids=true, to_apply=%region_5.6 | all-reduce | flops 12288 | bytes 98304 | tf_op jit(solution)/shard_map/psum | solution.py:49
  164.8 1.5 fusion.5
  166.3 0.6 copy.53
  (23 shorter events, 0.3 us)
Async XLA Ops:
  7.2 20.7 %reduce-scatter.2.cloned.1.call-start = ((), (), s32[]{:S(2)}) async-start(), calls=%async_computation.1 | async-start | bytes 98304 | tf_op jit(solution)/shard_map/reduce_scatter | solution.py:34
  9.5 1.3 copy-start
  10.8 0.8 copy-start.3
  11.6 0.7 copy-start.2
  13.0 0.7 copy-start.4
  13.0 0.7 copy-start.5
  94.8 6.7 %copy-start.1 = (f32[32,256]{1,0:T(8,128)S(1)}, f32[32,256]{1,0:T(8,128)}, u32[]{:S(2)}) copy-start(f32[32,256]{1,0:T(8,128)} %reduce-scatter.2.cloned.1.call-done) | copy-start | bytes 98308
Sparse Core Ops, SparseCore 0:
  15.2 12.5 reduce-scatter.1
